TPU v7x, 32 devices: a whole 2x2x4 slice. The times are simulated.
32 devices in a mesh: groups: 2 (over y), expert: 4 (over z), dp: 4 (over x, core).
Axes of the slice: x: 2, y: 2, z: 4, core: 2. Of those that a mesh axis runs over, the one named last changes fastest.
Arguments:
- out_grad: bfloat16 [4096, 2048], P(('groups', 'expert', 'dp')), parts along dimension 0, may hold values from -0.5 to 0.5
- gate_weights: bfloat16 [4096, 8], P(('groups', 'expert', 'dp')), parts along dimension 0, may hold values from 0.049804688 to 0.5
- expert_ids: int32 [4096, 8], P(('groups', 'expert', 'dp')), parts along dimension 0, may hold values from 0 to 31, all different within a row; in each aligned block of 128 rows (0 to 127, 128 to 255, ...) at most 36 rows name the same one
- hidden: bfloat16 [32, 8, 4, 36, 768], P('expert', ('groups', 'dp')), parts along dimension 1, may hold values from -6 to 6
- down_weight: bfloat16 [32, 768, 2048], P('expert', None, 'dp'), may hold values from -0.21875 to 0.21875
Outputs:
- weight_grad: float32 [64, 768, 2048], P(('groups', 'expert'), None, 'dp'), parts along dimension 0
- gate_grad: float32 [4096, 8], P(('groups', 'expert', 'dp')), parts along dimension 0
There are 2 independent parts, one for each index of `groups`. A program takes and returns all parts, laid end to end along the dimension named above; an argument that names none is the same for every part. Nothing has to cross between parts.
Inputs may be any that keep to these rules, and one draw needn't show every extreme that they name: `expert_ids`: each token names 8 different experts; within each block of 128 tokens (one device's tokens) no expert is named by more than 36 tokens, a bound that some block reaches.
All inputs are finite; a program needn't handle non-finite values.
Results may differ from a plain program's by a relative error of at most 0.0095.
Values may be sent and summed in bfloat16 or wider, within the bound.
No kernel may reach another device: no remote copies, remote signals or barrier semaphores. Data moves between devices by JAX's collectives and lax.ppermute only.
A program may use at most 128 MiB of HBM per device.

v0:
```python
import jax
import jax.numpy as jnp
from jax import lax
from jax.sharding import PartitionSpec as P


def per_device(out_grad, gate_weights, expert_ids, hidden, down_weight):
    tok_rows = out_grad.shape[0]
    top_count = expert_ids.shape[1]
    row_width = out_grad.shape[1]
    local_count = hidden.shape[0]
    peer_count = lax.axis_size("expert")
    expert_count = local_count * peer_count
    capacity = hidden.shape[3]
    hidden_width = hidden.shape[4]
    slot_rows = peer_count * capacity
    id_flat = expert_ids.reshape(-1)
    onehot = (id_flat[:, None] == jnp.arange(expert_count, dtype=jnp.int32)[None, :]).astype(
        jnp.int32
    )
    slot_index = jnp.sum((jnp.cumsum(onehot, axis=0) - 1) * onehot, axis=1)
    dest_index = id_flat * capacity + slot_index
    pair_count = tok_rows * top_count
    source_table = (
        jnp.full((expert_count * capacity,), pair_count, jnp.int32)
        .at[dest_index]
        .set(jnp.arange(pair_count, dtype=jnp.int32))
    )
    grad_ext = jnp.concatenate([out_grad, jnp.zeros((1, row_width), out_grad.dtype)], axis=0)
    gate_ext = jnp.concatenate(
        [gate_weights.reshape(-1), jnp.zeros((1,), gate_weights.dtype)], axis=0
    )
    send_grad = grad_ext[source_table // top_count].reshape(
        peer_count, local_count * capacity, row_width
    )
    send_gate = gate_ext[source_table].reshape(peer_count, local_count * capacity)
    recv_grad, recv_gate = (
        lax.all_to_all(send_grad, "expert", split_axis=0, concat_axis=0, tiled=True),
        lax.all_to_all(send_gate, "expert", split_axis=0, concat_axis=0, tiled=True),
    )
    recv_grad = recv_grad.reshape(peer_count, local_count, capacity, row_width).transpose(
        1, 0, 2, 3
    )
    recv_grad = recv_grad.reshape(local_count, slot_rows, row_width)
    recv_gate = recv_gate.reshape(peer_count, local_count, capacity).transpose(1, 0, 2)
    recv_gate = recv_gate.reshape(local_count, slot_rows)
    scaled = (recv_gate.astype(jnp.float32)[:, :, None] * recv_grad).astype(jnp.bfloat16)
    hidden_rows = hidden.reshape(local_count, slot_rows, hidden_width)
    shards = lax.axis_size("dp")
    column_part = scaled.reshape(local_count, slot_rows, shards, row_width // shards)
    columns_in = lax.all_to_all(column_part, "dp", split_axis=2, concat_axis=2, tiled=True)
    hidden_all = lax.all_gather(hidden_rows[:, None], "dp", axis=1, tiled=True)
    partial_value = jnp.einsum(
        "eirf,erid->eifd", hidden_all, columns_in, preferred_element_type=jnp.float32
    ).astype(jnp.bfloat16)
    weight_grad = jnp.sum(partial_value.astype(jnp.float32), axis=1)
    full_weight = lax.all_gather(down_weight, "dp", axis=2, tiled=True)
    expert_out = jnp.einsum(
        "erf,efd->erd", hidden_rows, full_weight, preferred_element_type=jnp.float32
    )
    slot_grad = jnp.sum(recv_grad * expert_out, axis=2)
    send_back = slot_grad.reshape(local_count, peer_count, capacity).transpose(1, 0, 2)
    send_back = send_back.reshape(peer_count, local_count * capacity)
    returned = lax.all_to_all(send_back, "expert", split_axis=0, concat_axis=0, tiled=True)
    gate_grad = returned.reshape(-1)[dest_index].reshape(tok_rows, top_count)
    return (weight_grad, gate_grad)


def solution(mesh):
    return jax.shard_map(
        per_device,
        mesh=mesh,
        in_specs=(
            P(("groups", "expert", "dp"), None),
            P(("groups", "expert", "dp"), None),
            P(("groups", "expert", "dp"), None),
            P("expert", ("groups", "dp"), None, None, None),
            P("expert", None, "dp"),
        ),
        out_specs=(P(("groups", "expert"), None, "dp"), P(("groups", "expert", "dp"), None)),
        check_vma=False,
    )
```

profile of v0, /device:TPU:0, one launch (start us, length us, event | category | flops | bytes accessed | tf_op | source)
XLA Modules:
  0.0 316.2 jit_solution(5351354100891161966)
XLA Ops:
  7.2 0.7 all-gather.5.cloned.1.call-update
  7.9 0.8 copy.44
  8.9 9.0 %reduce-window.6 = s32[32,8,128]{2,1,0:T(8,128)S(1)} reduce-window(s32[32,8,128]{2,1,0:T(8,128)S(1)} %fusion.5, s32[]{:T(128)} %constant.16.clone.1), window={size=1x1x128 pad=0_0x0_0x127_0}, to_apply=%region_0.0 | reduce-window | flops 4161536 | bytes 262148 | tf_op jit(solution)/shard_map/reduce-window
  18.0 0.1 copy.46
  18.5 0.1 copy.42
  18.9 4.3 %scatter_custom_fusion = s32[1152]{0:T(1024)S(1)} fusion(s32[1024]{0:T(1024)S(1)} %bitcast.43, s32[1024]{0:T(1024)S(1)} %iota.11, s32[]{:T(128)} %constant.12.clone.1), kind=kCustom, calls=%fused_computation.31 | custom fusion | bytes 4612 | tf_op jit(solution)/shard_map/scatter | solution.py:27
  23.3 7.3 %gather_fusion = bf16[1152]{0:T(1024)(128)(2,1)S(1)} fusion(bf16[1025]{0:T(1024)(128)(2,1)S(1)} %pad_maximum_fusion, s32[2048]{0:T(1024)S(1)} %get-tuple-element.11), kind=kCustom, calls=%fused_computation | custom fusion | bytes 9216 | tf_op jit(solution)/shard_map/gather | solution.py:36
  30.7 0.5 broadcast.92
  31.2 0.7 reduce.4
  31.8 0.7 reshape.154
  32.5 6.3 %all-to-all-start = ((bf16[4,2,144]{2,1,0:T(2,128)(2,1)}), bf16[4,2,144]{2,1,0:T(2,128)(2,1)S(1)}, u32[]{:S(2)}, u32[]{:S(2)}) async-start(bf16[4,2,144]{2,1,0:T(2,128)(2,1)} %reshape.154), calls=%async_computation | async-start | bytes 8192 | tf_op jit(solution)/shard_map/all_to_all | solution.py:39
  38.9 5.9 %gather_fusion.1 = bf16[1152,2048]{1,0:T(8,128)(2,1)} fusion(bf16[129,2048]{1,0:T(8,128)(2,1)S(1)} %concatenate.7, s32[2048]{0:T(1024)S(1)} %get-tuple-element.10), kind=kCustom, calls=%fused_computation.1 | custom fusion | bytes 9441792 | tf_op jit(solution)/shard_map/gather | solution.py:33
  44.8 5.2 %all-to-all-start.1 = ((bf16[4,288,2048]{2,1,0:T(8,128)(2,1)}), bf16[4,288,2048]{2,1,0:T(8,128)(2,1)}, u32[]{:S(2)}, u32[]{:S(2)}) async-start(bf16[4,288,2048]{2,1,0:T(8,128)(2,1)} %bitcast.34), calls=%async_computation.1 | async-start | bytes 9437184 | tf_op jit(solution)/shard_map/all_to_all | solution.py:38
  50.0 0.2 all-gather.3.cloned.1.call-start
  50.2 0.5 copy.54
  50.8 1.2 copy-done
  52.0 1.6 copy.55
  53.9 100.5 %all-to-all-done.1 = bf16[4,288,2048]{2,1,0:T(8,128)(2,1)} async-done(((bf16[4,288,2048]{2,1,0:T(8,128)(2,1)}), bf16[4,288,2048]{2,1,0:T(8,128)(2,1)}, u32[]{:S(2)}, u32[]{:S(2)}) %all-to-all-start.1) | async-done | bytes 4718624 | tf_op jit(solution)/shard_map/all_to_all | solution.py:38
  154.4 6.0 %copy.51 = f32[4,288,2048]{2,0,1:T(4,128)S(1)} copy(bf16[4,288,2048]{2,1,0:T(8,128)(2,1)} %all-to-all-done.1) | data formatting | bytes 14155776 | tf_op jit(solution)/shard_map/convert_element_type | solution.py:47
  160.4 9.2 %copy.52 = f32[8,4,36,2048]{3,0,2,1:T(8,128)} copy(f32[8,4,36,2048]{3,1,2,0:T(4,128)S(1)} %bitcast.33) | data formatting | bytes 18874368 | tf_op jit(solution)/shard_map/convert_element_type | solution.py:47
  169.6 12.6 %reshape.111 = f32[8,144,4,512]{3,2,0,1:T(4,128)} reshape(f32[8,4,36,2048]{3,0,2,1:T(8,128)} %copy.52) | data formatting | bytes 18874368 | tf_op jit(solution)/shard_map/convert_element_type | solution.py:47
  182.2 6.1 %multiply_convert_fusion = bf16[8,144,4,512]{3,2,0,1:T(4,128)(2,1)S(1)} fusion(f32[8,144,4,512]{3,2,0,1:T(4,128)} %reshape.111, f32[8,144]{0,1:T(8,128)S(1)} %copy.50), kind=kLoop, calls=%fused_computation.7 | loop fusion | flops 4718592 | bytes 14160384 | tf_op jit(solution)/shard_map/convert_element_type | solution.py:47
  188.2 4.8 %copy.53 = bf16[8,144,4,512]{3,1,0,2:T(8,128)(2,1)} copy(bf16[8,144,4,512]{3,2,0,1:T(4,128)(2,1)S(1)} %multiply_convert_fusion) | data formatting | bytes 9437184 | tf_op jit(solution)/shard_map/convert_element_type | solution.py:47
  193.0 5.2 %all-to-all-start.2 = ((bf16[8,144,4,512]{3,1,0,2:T(8,128)(2,1)}), bf16[8,144,4,512]{3,1,0,2:T(8,128)(2,1)}, u32[]{:S(2)}, u32[]{:S(2)}) async-start(bf16[8,144,4,512]{3,1,0,2:T(8,128)(2,1)} %copy.53), calls=%async_computation.2 | async-start | bytes 9437184 | tf_op jit(solution)/shard_map/all_to_all | solution.py:51
  198.3 20.2 %fusion = f32[8,144]{1,0:T(8,128)S(1)} fusion(f32[8,144,2048]{2,0,1:T(8,128)} %bitcast.32, bf16[8,768,2048]{2,1,0:T(8,128)(2,1)} %all-gather.5.cloned.1.call-done, bf16[8,144,768]{2,0,1:T(8,128)(2,1)S(1)} %bitcast.36), kind=kOutput, calls=%fused_computation.6 | convolution fusion | flops 3628596224 | bytes 36377088 | tf_op jit(solution)/shard_map/erf,efd->erd/dot_general | solution.py:58
  218.6 0.7 all_to_all.25
  219.3 49.3 %all-to-all-done.2 = bf16[8,144,4,512]{3,1,0,2:T(8,128)(2,1)} async-done(((bf16[8,144,4,512]{3,1,0,2:T(8,128)(2,1)}), bf16[8,144,4,512]{3,1,0,2:T(8,128)(2,1)}, u32[]{:S(2)}, u32[]{:S(2)}) %all-to-all-start.2) | async-done | bytes 4718624 | tf_op jit(solution)/shard_map/all_to_all | solution.py:51
  268.6 4.6 %all-to-all-start.3 = ((f32[4,1,288]{2,1,0:T(1,128)}), f32[4,1,288]{2,1,0:T(1,128)S(1)}, u32[]{:S(2)}, u32[]{:S(2)}) async-start(f32[4,1,288]{2,1,0:T(1,128)} %all_to_all.25), calls=%async_computation.3 | async-start | bytes 12288 | tf_op jit(solution)/shard_map/all_to_all | solution.py:64
  273.2 16.6 %convert_reduce_fusion = f32[8,512,768]{2,1,0:T(8,128)} fusion(bf16[8,4,144,768]{3,2,1,0:T(8,128)(2,1)} %all-gather.3.cloned.1.call-done, bf16[8,144,4,512]{3,1,0,2:T(8,128)(2,1)} %all-to-all-done.2), kind=kOutput, calls=%fused_computation.4 | convolution fusion | flops 3658481664 | bytes 24379392 | tf_op jit(solution)/shard_map/eirf,erid->eifd/dot_general | solution.py:53
  289.7 12.6 %copy.63 = f32[8,768,512]{2,1,0:T(8,128)} copy(f32[8,768,512]{1,2,0:T(8,128)} %bitcast.37) | data formatting | bytes 25165824
  302.4 6.2 %gather_fusion.2 = f32[1024]{0:T(1024)S(1)} fusion(f32[1152]{0:T(1024)S(1)} %reshape.108, s32[1024]{0:T(1024)S(1)} %broadcast_clamp_fusion), kind=kCustom, calls=%fused_computation.2 | custom fusion | bytes 12288 | tf_op jit(solution)/shard_map/gather | solution.py:65
  308.7 0.7 copy.64
  (49 shorter events, 1.8 us)
Async XLA Ops:
  7.2 11.1 %copy-start.4 = (s32[128,8]{0,1:T(8,128)S(1)}, s32[128,8]{0,1:T(8,128)}, u32[]{:S(2)}) copy-start(s32[128,8]{0,1:T(8,128)} %param.7) | copy-start | bytes 12292
  7.2 11.3 %copy-start.5 = (bf16[128,8]{0,1:T(8,128)(2,1)S(1)}, bf16[128,8]{0,1:T(8,128)(2,1)}, u32[]{:S(2)}) copy-start(bf16[128,8]{0,1:T(8,128)(2,1)} %param.6) | copy-start | bytes 6148
  7.2 31.7 %copy-start.3 = (bf16[128,2048]{1,0:T(8,128)(2,1)S(1)}, bf16[128,2048]{1,0:T(8,128)(2,1)}, u32[]{:S(2)}) copy-start(bf16[128,2048]{1,0:T(8,128)(2,1)} %param.5) | copy-start | bytes 1572868
  7.2 191.1 %all-gather.5.cloned.1.call-start = ((), (), s32[]{:S(2)}) async-start(), calls=%async_computation.5 | async-start | bytes 31457280 | tf_op jit(solution)/shard_map/all_gather | solution.py:57
  32.5 12.3 %all-to-all-start = ((bf16[4,2,144]{2,1,0:T(2,128)(2,1)}), bf16[4,2,144]{2,1,0:T(2,128)(2,1)S(1)}, u32[]{:S(2)}, u32[]{:S(2)}) async-start(bf16[4,2,144]{2,1,0:T(2,128)(2,1)} %reshape.154), calls=%async_computation | async-start | bytes 8192 | tf_op jit(solution)/shard_map/all_to_all | solution.py:39
  44.8 5.4 %copy-start.2 = (bf16[8,1,4,36,768]{4,2,3,1,0:T(4,128)(2,1)S(1)}, bf16[8,1,4,36,768]{4,2,3,1,0:T(4,128)(2,1)}, u32[]{:S(2)}) copy-start(bf16[8,1,4,36,768]{4,2,3,1,0:T(4,128)(2,1)} %param.8) | copy-start | bytes 5308420
  44.8 109.6 %all-to-all-start.1 = ((bf16[4,288,2048]{2,1,0:T(8,128)(2,1)}), bf16[4,288,2048]{2,1,0:T(8,128)(2,1)}, u32[]{:S(2)}, u32[]{:S(2)}) async-start(bf16[4,288,2048]{2,1,0:T(8,128)(2,1)} %bitcast.34), calls=%async_computation.1 | async-start | bytes 9437184 | tf_op jit(solution)/shard_map/all_to_all | solution.py:38
  50.0 223.1 %all-gather.3.cloned.1.call-start = ((), (), s32[]{:S(2)}) async-start(), calls=%async_computation.4 | async-start | bytes 8847360 | tf_op jit(solution)/shard_map/all_gather | solution.py:52
  50.8 1.2 copy-start
  193.0 5.2 %copy-start.1 = (bf16[8,1,4,36,768]{4,0,3,2,1:T(8,128)(2,1)S(1)}, bf16[8,1,4,36,768]{4,0,3,2,1:T(8,128)(2,1)}, u32[]{:S(2)}) copy-start(bf16[8,1,4,36,768]{4,0,3,2,1:T(8,128)(2,1)} %copy-done) | copy-start | bytes 5308420
  193.0 75.5 %all-to-all-start.2 = ((bf16[8,144,4,512]{3,1,0,2:T(8,128)(2,1)}), bf16[8,144,4,512]{3,1,0,2:T(8,128)(2,1)}, u32[]{:S(2)}, u32[]{:S(2)}) async-start(bf16[8,144,4,512]{3,1,0,2:T(8,128)(2,1)} %copy.53), calls=%async_computation.2 | async-start | bytes 9437184 | tf_op jit(solution)/shard_map/all_to_all | solution.py:51
  268.6 33.8 %all-to-all-start.3 = ((f32[4,1,288]{2,1,0:T(1,128)}), f32[4,1,288]{2,1,0:T(1,128)S(1)}, u32[]{:S(2)}, u32[]{:S(2)}) async-start(f32[4,1,288]{2,1,0:T(1,128)} %all_to_all.25), calls=%async_computation.3 | async-start | bytes 12288 | tf_op jit(solution)/shard_map/all_to_all | solution.py:64
Sparse Core Ops, SparseCore 0:
  9.6 157.5 all-gather.4
  168.7 67.3 all-gather.2
where the time goes:
time: 317 us; the launch traced here: 316 us
  waiting for transfers between devices  150 us (47%)
  local copies, waits for them, and re-layouts  77.1 us (24%)
  matrix products  36.8 us (12%)
  starting transfers between devices  21.5 us (7%)
  other arithmetic  16 us (5%)
  between operations  14.3 us (5%)
    all_to_all x1, waiting for transfers between devices, per_device(): lax.all_to_all(send_grad, 'expert', split_axis=0, concat_axis=0, tiled=True)  100 us
    all_to_all x1, waiting for transfers between devices, per_device(): lax.all_to_all(column_part, 'dp', split_axis=2, concat_axis=2, tiled=True)  49.3 us
    convert_element_type x7, local copies, waits for them, and re-layouts, per_device(): recv_gate.astype(jnp.float32)[:, :, None] * recv_grad  28 us
    dot_general x1, matrix products, per_device(): jnp.einsum('erf,efd->erd', hidden_rows, full_weight, preferred_element_ty...  20.2 us
    unnamed x19, local copies, waits for them, and re-layouts  16.7 us
    dot_general x1, matrix products, per_device(): jnp.einsum('eirf,erid->eifd', hidden_all, columns_in, preferred_element_t...  16.6 us
    another operation x2, other arithmetic  9.04 us
    gather x1, local copies, waits for them, and re-layouts, per_device(): gate_ext[source_table].reshape(peer_count, local_count * capacity)  7.27 us
  transfers between devices with their start and end apart: 6, of which 2 were waited for; matrix products, arithmetic and copies ran while one was open for 38% of the time, Pallas kernels for 0%

commit v1 on v0

--- a/solution.py
+++ b/solution.py
@@ -48,7 +48,10 @@
     hidden_rows = hidden.reshape(local_count, slot_rows, hidden_width)
     shards = lax.axis_size("dp")
     column_part = scaled.reshape(local_count, slot_rows, shards, row_width // shards)
-    columns_in = lax.all_to_all(column_part, "dp", split_axis=2, concat_axis=2, tiled=True)
+    columns_in = jnp.concatenate(
+        lax.all_to_all(jnp.stack(jnp.split(column_part, lax.axis_size("dp"), axis=2)), "dp", 0, 0),
+        axis=2,
+    )
     hidden_all = lax.all_gather(hidden_rows[:, None], "dp", axis=1, tiled=True)
     partial_value = jnp.einsum(
         "eirf,erid->eifd", hidden_all, columns_in, preferred_element_type=jnp.float32

time: 317 us -> 321 us (1.013); the launches traced: 316 us -> 317 us
  waiting for transfers between devices: 150 us -> 137 us
  local copies, waits for them, and re-layouts: 77.1 us -> 87.9 us
    split x0 -> x5, local copies, waits for them, and re-layouts: none -> 15.7 us  [per_device(): jnp.split(column_part, lax.axis_size('dp'), axis=2)]
    all_to_all x1, waiting for transfers between devices: 49.3 us -> 35.8 us  [per_device(): lax.all_to_all(jnp.stack(jnp.split(column_part, lax.axis_size('dp'), axis...]
    convert_element_type x1 -> x0, local copies, waits for them, and re-layouts: 4.8 us -> none  [per_device(): (recv_gate.astype(jnp.float32)[:, :, None] * recv_grad).astype(jnp.bfloat16)]
    another operation x2 -> x3, other arithmetic: 9.04 us -> 11.5 us
  transfers between devices with their start and end apart: 6 -> 6, of which waited for: 2 -> 2; matrix products, arithmetic and copies ran while one was open for 38% -> 42% of each run, Pallas kernels for 0% -> 0%
where the time goes in v1:
time: 321 us; the launch traced here: 317 us
  waiting for transfers between devices  137 us (43%)
  local copies, waits for them, and re-layouts  87.9 us (27%)
  matrix products  36.8 us (11%)
  starting transfers between devices  22 us (7%)
  other arithmetic  18.5 us (6%)
  between operations  14.6 us (5%)
    all_to_all x1, waiting for transfers between devices, per_device(): lax.all_to_all(send_grad, 'expert', split_axis=0, concat_axis=0, tiled=True)  100 us
    all_to_all x1, waiting for transfers between devices, per_device(): lax.all_to_all(jnp.stack(jnp.split(column_part, lax.axis_size('dp'), axis...  35.8 us
    convert_element_type x7, local copies, waits for them, and re-layouts, per_device(): recv_gate.astype(jnp.float32)[:, :, None] * recv_grad  28.6 us
    dot_general x1, matrix products, per_device(): jnp.einsum('erf,efd->erd', hidden_rows, full_weight, preferred_element_ty...  20.2 us
    dot_general x1, matrix products, per_device(): jnp.einsum('eirf,erid->eifd', hidden_all, columns_in, preferred_element_t...  16.6 us
    unnamed x19, local copies, waits for them, and re-layouts  16 us
    split x5, local copies, waits for them, and re-layouts, per_device(): jnp.split(column_part, lax.axis_size('dp'), axis=2)  15.7 us
    another operation x2, other arithmetic  9.04 us
  transfers between devices with their start and end apart: 6, of which 2 were waited for; matrix products, arithmetic and copies ran while one was open for 42% of the time, Pallas kernels for 0%

profile of v1, /device:TPU:0, one launch (start us, length us, event | category | flops | bytes accessed | tf_op | source)
XLA Modules:
  0.0 316.7 jit_solution(3216414738815729904)
XLA Ops:
  7.2 0.7 all-gather.5.cloned.1.call-update
  8.2 9.0 %reduce-window.6 = s32[32,8,128]{2,1,0:T(8,128)S(1)} reduce-window(s32[32,8,128]{2,1,0:T(8,128)S(1)} %fusion.6, s32[]{:T(128)} %constant.16.clone.1), window={size=1x1x128 pad=0_0x0_0x127_0}, to_apply=%region_0.0 | reduce-window | flops 4161536 | bytes 262148 | tf_op jit(solution)/shard_map/reduce-window
  18.2 4.3 %scatter_custom_fusion = s32[1152]{0:T(1024)S(1)} fusion(s32[1024]{0:T(1024)S(1)} %bitcast.64, s32[1024]{0:T(1024)S(1)} %iota.11, s32[]{:T(128)} %constant.12.clone.1), kind=kCustom, calls=%fused_computation.37 | custom fusion | bytes 4612 | tf_op jit(solution)/shard_map/scatter | solution.py:27
  22.6 7.3 %gather_fusion = bf16[1152]{0:T(1024)(128)(2,1)S(1)} fusion(bf16[1025]{0:T(1024)(128)(2,1)S(1)} %pad_maximum_fusion.1, s32[2048]{0:T(1024)S(1)} %get-tuple-element.23), kind=kCustom, calls=%fused_computation | custom fusion | bytes 9216 | tf_op jit(solution)/shard_map/gather | solution.py:36
  30.5 0.7 reduce.4
  31.2 0.7 reshape.162
  31.8 6.3 %all-to-all-start = ((bf16[4,2,144]{2,1,0:T(2,128)(2,1)}), bf16[4,2,144]{2,1,0:T(2,128)(2,1)S(1)}, u32[]{:S(2)}, u32[]{:S(2)}) async-start(bf16[4,2,144]{2,1,0:T(2,128)(2,1)} %reshape.162), calls=%async_computation | async-start | bytes 8192 | tf_op jit(solution)/shard_map/all_to_all | solution.py:39
  38.2 5.9 %gather_fusion.1 = bf16[1152,2048]{1,0:T(8,128)(2,1)} fusion(bf16[129,2048]{1,0:T(8,128)(2,1)S(1)} %concatenate.7, s32[2048]{0:T(1024)S(1)} %get-tuple-element.22), kind=kCustom, calls=%fused_computation.1 | custom fusion | bytes 9441792 | tf_op jit(solution)/shard_map/gather | solution.py:33
  44.1 5.2 %all-to-all-start.1 = ((bf16[4,288,2048]{2,1,0:T(8,128)(2,1)}), bf16[4,288,2048]{2,1,0:T(8,128)(2,1)}, u32[]{:S(2)}, u32[]{:S(2)}) async-start(bf16[4,288,2048]{2,1,0:T(8,128)(2,1)} %bitcast.51), calls=%async_computation.1 | async-start | bytes 9437184 | tf_op jit(solution)/shard_map/all_to_all | solution.py:38
  49.7 0.5 copy.177
  50.2 1.2 copy-done
  51.4 1.6 copy.178
  53.4 100.3 %all-to-all-done.1 = bf16[4,288,2048]{2,1,0:T(8,128)(2,1)} async-done(((bf16[4,288,2048]{2,1,0:T(8,128)(2,1)}), bf16[4,288,2048]{2,1,0:T(8,128)(2,1)}, u32[]{:S(2)}, u32[]{:S(2)}) %all-to-all-start.1) | async-done | bytes 4718624 | tf_op jit(solution)/shard_map/all_to_all | solution.py:38
  153.7 6.0 %copy.170 = f32[4,288,2048]{2,0,1:T(4,128)S(1)} copy(bf16[4,288,2048]{2,1,0:T(8,128)(2,1)} %all-to-all-done.1) | data formatting | bytes 14155776 | tf_op jit(solution)/shard_map/convert_element_type | solution.py:47
  159.7 9.2 %copy.171 = f32[8,4,36,2048]{3,0,2,1:T(8,128)} copy(f32[8,4,36,2048]{3,1,2,0:T(4,128)S(1)} %bitcast.50) | data formatting | bytes 18874368 | tf_op jit(solution)/shard_map/convert_element_type | solution.py:47
  168.9 13.2 %reshape.119 = f32[8,144,4,512]{3,2,0,1:T(4,128)} reshape(f32[8,4,36,2048]{3,0,2,1:T(8,128)} %copy.171) | data formatting | bytes 18874368 | tf_op jit(solution)/shard_map/convert_element_type | solution.py:47
  182.1 6.1 %multiply_convert_fusion = bf16[8,144,4,512]{3,2,0,1:T(4,128)(2,1)S(1)} fusion(f32[8,144,4,512]{3,2,0,1:T(4,128)} %reshape.119, f32[8,144]{0,1:T(8,128)S(1)} %copy.169), kind=kLoop, calls=%fused_computation.7 | loop fusion | flops 4718592 | bytes 14160384 | tf_op jit(solution)/shard_map/convert_element_type | solution.py:47
  188.2 10.7 %fusion.11 = (bf16[8,144,1,512]{3,2,0,1:T(2,128)(2,1)S(1)}, bf16[8,144,1,512]{3,2,0,1:T(2,128)(2,1)S(1)}, bf16[8,144,1,512]{3,2,0,1:T(2,128)(2,1)S(1)}, bf16[8,144,1,512]{3,2,0,1:T(2,128)(2,1)S(1)}) fusion(bf16[8,144,4,512]{3,2,0,1:T(4,128)(2,1)S(1)} %multiply_convert_fusion), kind=kLoop, calls=%fused_computation.41 | loop fusion | bytes 9437184 | tf_op jit(solution)/shard_map/split | solution.py:52
  198.8 1.3 copy.202
  200.1 1.3 copy.203
  201.4 1.3 copy.204
  202.6 1.3 copy.205
  203.9 2.5 pad_maximum_fusion
  206.3 5.3 %all-to-all-start.2 = ((bf16[4,8,144,1,512]{4,2,1,3,0:T(8,128)(2,1)}), bf16[4,8,144,1,512]{4,2,1,3,0:T(8,128)(2,1)}, u32[]{:S(2)}, u32[]{:S(2)}) async-start(bf16[4,8,144,1,512]{4,2,1,3,0:T(8,128)(2,1)} %pad_maximum_fusion), calls=%async_computation.2 | async-start | bytes 9437184 | tf_op jit(solution)/shard_map/all_to_all | solution.py:52
  211.7 20.2 %fusion = f32[8,144]{1,0:T(8,128)S(1)} fusion(f32[8,144,2048]{2,0,1:T(8,128)} %bitcast.49, bf16[8,768,2048]{2,1,0:T(8,128)(2,1)} %all-gather.5.cloned.1.call-done, bf16[8,144,768]{2,0,1:T(8,128)(2,1)S(1)} %bitcast.53), kind=kOutput, calls=%fused_computation.6 | convolution fusion | flops 3628596224 | bytes 36377088 | tf_op jit(solution)/shard_map/erf,efd->erd/dot_general | solution.py:61
  232.1 0.7 all_to_all.25
  232.8 35.8 %all-to-all-done.2 = bf16[4,8,144,1,512]{4,2,1,3,0:T(8,128)(2,1)} async-done(((bf16[4,8,144,1,512]{4,2,1,3,0:T(8,128)(2,1)}), bf16[4,8,144,1,512]{4,2,1,3,0:T(8,128)(2,1)}, u32[]{:S(2)}, u32[]{:S(2)}) %all-to-all-start.2) | async-done | bytes 4718624 | tf_op jit(solution)/shard_map/all_to_all | solution.py:52
  268.5 4.8 %all-to-all-start.3 = ((f32[4,1,288]{2,1,0:T(1,128)}), f32[4,1,288]{2,1,0:T(1,128)S(1)}, u32[]{:S(2)}, u32[]{:S(2)}) async-start(f32[4,1,288]{2,1,0:T(1,128)} %all_to_all.25), calls=%async_computation.3 | async-start | bytes 12288 | tf_op jit(solution)/shard_map/all_to_all | solution.py:67
  273.4 16.6 %convert_reduce_fusion = f32[8,512,768]{2,1,0:T(8,128)} fusion(bf16[8,4,144,768]{3,2,1,0:T(8,128)(2,1)} %all-gather.3.cloned.1.call-done, bf16[4,8,144,1,512]{4,2,1,3,0:T(8,128)(2,1)} %all-to-all-done.2), kind=kOutput, calls=%fused_computation.4 | convolution fusion | flops 3658481664 | bytes 24379392 | tf_op jit(solution)/shard_map/eirf,erid->eifd/dot_general | solution.py:56
  290.0 12.6 %copy.185 = f32[8,768,512]{2,1,0:T(8,128)} copy(f32[8,768,512]{1,2,0:T(8,128)} %bitcast.54) | data formatting | bytes 25165824
  302.7 6.2 %gather_fusion.2 = f32[1024]{0:T(1024)S(1)} fusion(f32[1152]{0:T(1024)S(1)} %reshape.116, s32[1024]{0:T(1024)S(1)} %broadcast_clamp_fusion), kind=kCustom, calls=%fused_computation.2 | custom fusion | bytes 12288 | tf_op jit(solution)/shard_map/gather | solution.py:68
  308.9 0.7 copy.186
  (54 shorter events, 2.9 us)
Async XLA Ops:
  7.2 0.8 copy-start.4
  7.2 10.6 %copy-start.5 = (bf16[128,8]{0,1:T(8,128)(2,1)S(1)}, bf16[128,8]{0,1:T(8,128)(2,1)}, u32[]{:S(2)}) copy-start(bf16[128,8]{0,1:T(8,128)(2,1)} %param.6) | copy-start | bytes 6148
  7.2 31.0 %copy-start.3 = (bf16[128,2048]{1,0:T(8,128)(2,1)S(1)}, bf16[128,2048]{1,0:T(8,128)(2,1)}, u32[]{:S(2)}) copy-start(bf16[128,2048]{1,0:T(8,128)(2,1)} %param.5) | copy-start | bytes 1572868
  7.2 204.5 %all-gather.5.cloned.1.call-start = ((), (), s32[]{:S(2)}) async-start(), calls=%async_computation.5 | async-start | bytes 31457280 | tf_op jit(solution)/shard_map/all_gather | solution.py:60
  31.8 12.3 %all-to-all-start = ((bf16[4,2,144]{2,1,0:T(2,128)(2,1)}), bf16[4,2,144]{2,1,0:T(2,128)(2,1)S(1)}, u32[]{:S(2)}, u32[]{:S(2)}) async-start(bf16[4,2,144]{2,1,0:T(2,128)(2,1)} %reshape.162), calls=%async_computation | async-start | bytes 8192 | tf_op jit(solution)/shard_map/all_to_all | solution.py:39
  44.1 5.5 %copy-start.2 = (bf16[8,1,4,36,768]{4,2,3,1,0:T(4,128)(2,1)S(1)}, bf16[8,1,4,36,768]{4,2,3,1,0:T(4,128)(2,1)}, u32[]{:S(2)}) copy-start(bf16[8,1,4,36,768]{4,2,3,1,0:T(4,128)(2,1)} %param.8) | copy-start | bytes 5308420
  44.1 109.6 %all-to-all-start.1 = ((bf16[4,288,2048]{2,1,0:T(8,128)(2,1)}), bf16[4,288,2048]{2,1,0:T(8,128)(2,1)}, u32[]{:S(2)}, u32[]{:S(2)}) async-start(bf16[4,288,2048]{2,1,0:T(8,128)(2,1)} %bitcast.51), calls=%async_computation.1 | async-start | bytes 9437184 | tf_op jit(solution)/shard_map/all_to_all | solution.py:38
  49.4 224.0 %all-gather.3.cloned.1.call-start = ((), (), s32[]{:S(2)}) async-start(), calls=%async_computation.4 | async-start | bytes 8847360 | tf_op jit(solution)/shard_map/all_gather | solution.py:55
  50.2 1.2 copy-start
  206.3 5.4 %copy-start.1 = (bf16[8,1,4,36,768]{4,0,3,2,1:T(8,128)(2,1)S(1)}, bf16[8,1,4,36,768]{4,0,3,2,1:T(8,128)(2,1)}, u32[]{:S(2)}) copy-start(bf16[8,1,4,36,768]{4,0,3,2,1:T(8,128)(2,1)} %copy-done) | copy-start | bytes 5308420
  206.3 62.2 %all-to-all-start.2 = ((bf16[4,8,144,1,512]{4,2,1,3,0:T(8,128)(2,1)}), bf16[4,8,144,1,512]{4,2,1,3,0:T(8,128)(2,1)}, u32[]{:S(2)}, u32[]{:S(2)}) async-start(bf16[4,8,144,1,512]{4,2,1,3,0:T(8,128)(2,1)} %pad_maximum_fusion), calls=%async_computation.2 | async-start | bytes 9437184 | tf_op jit(solution)/shard_map/all_to_all | solution.py:52
  268.5 34.0 %all-to-all-start.3 = ((f32[4,1,288]{2,1,0:T(1,128)}), f32[4,1,288]{2,1,0:T(1,128)S(1)}, u32[]{:S(2)}, u32[]{:S(2)}) async-start(f32[4,1,288]{2,1,0:T(1,128)} %all_to_all.25), calls=%async_computation.3 | async-start | bytes 12288 | tf_op jit(solution)/shard_map/all_to_all | solution.py:67
Sparse Core Ops, SparseCore 0:
  9.6 157.4 all-gather.4
  168.7 53.9 all-gather.2
